TPU v7x, 512 devices: a whole 4x4x16 slice. The times are simulated.
512 devices in a mesh: dp: 16 (over z), owner: 32 (over x, y, core).
Axes of the slice: x: 4, y: 4, z: 16, core: 2. Of those that a mesh axis runs over, the one named last changes fastest.
Arguments:
- tokens: bfloat16 [65536, 8192], P(('dp', 'owner')), may hold values from -6 to 6
- residual: bfloat16 [65536, 8192], P(('dp', 'owner')), may hold values from -6 to 6
- token_adapter_index: int32 [65536, 1], P(('dp', 'owner')), may hold values from 0 to 31; in each aligned block of 128 rows (0 to 127, 128 to 255, ...) at most 6 rows name the same one
- adapter_down_weight: bfloat16 [32, 64, 8192], P('owner', None, 'dp'), may hold values from -0.0625 to 0.0625
- adapter_up_weight: bfloat16 [32, 64, 8192], P('owner', None, 'dp'), may hold values from -0.75 to 0.75
- down_moment_first: bfloat16 [32, 64, 8192], P('owner', None, 'dp'), may hold values from -270 to 270
- down_moment_second: bfloat16 [32, 64, 8192], P('owner', None, 'dp'), may hold values from 816 to 24576
- up_moment_first: bfloat16 [32, 64, 8192], P('owner', None, 'dp'), may hold values from -27.125 to 27.125
- up_moment_second: bfloat16 [32, 64, 8192], P('owner', None, 'dp'), may hold values from 6.125 to 204
Outputs:
- down_update: float32 [32, 64, 8192], P('owner', None, 'dp')
- up_update: float32 [32, 64, 8192], P('owner', None, 'dp')
- token_loss: float32 [65536], P(('dp', 'owner'))
Inputs may be any that keep to these rules, and one draw needn't show every extreme that they name: `token_adapter_index`: of the 128 rows of one device, at most 6 name one adapter, and in some devices one adapter is named by exactly 6.
All inputs are finite; a program needn't handle non-finite values.
Results may differ from a plain program's by a relative error of at most 0.0091.
Values may be sent and summed in bfloat16 or wider, within the bound.
No kernel may reach another device: no remote copies, remote signals or barrier semaphores. Data moves between devices by JAX's collectives and lax.ppermute only.
A program may use at most 128 MiB of HBM per device.

v0:
```python
import jax
import jax.numpy as jnp
from jax import lax
from jax.sharding import PartitionSpec as P

adapter_scale = 0.5
adam_eps = 1e-08


def adam_update(grad, first, second):
    first_new = 0.9 * first.astype(jnp.float32) + 0.1 * grad
    second_new = 0.95 * second.astype(jnp.float32) + 0.05 * grad * grad
    return first_new / (jnp.sqrt(second_new) + adam_eps)


def body(
    tokens,
    residual,
    token_adapter_index,
    adapter_down_weight,
    adapter_up_weight,
    down_moment_first,
    down_moment_second,
    up_moment_first,
    up_moment_second,
):
    owner_index = lax.axis_size("owner")
    tok_rows = tokens.shape[0]
    model_width_value = tokens.shape[1]
    column_span = adapter_down_weight.shape[2]
    slot_capacity = max(2, 3 * tok_rows // (2 * owner_index))
    route_ids = token_adapter_index[:, 0]
    member = (route_ids[:, None] == jnp.arange(owner_index, dtype=jnp.int32)[None, :]).astype(
        jnp.int32
    )
    before = jnp.cumsum(member, axis=0) - member
    within = jnp.sum(before * member, axis=1)
    target = route_ids * slot_capacity + within
    dispatch = (
        jnp.arange(owner_index * slot_capacity, dtype=jnp.int32)[:, None] == target[None, :]
    ).astype(jnp.bfloat16)

    def placed_rows(row_block):
        return jnp.dot(dispatch, row_block, preferred_element_type=jnp.float32).astype(jnp.bfloat16)

    down_full, up_weight_whole = (
        lax.all_gather(adapter_down_weight, "dp", axis=2, tiled=True),
        lax.all_gather(adapter_up_weight, "dp", axis=2, tiled=True),
    )
    down_full = down_full[0]
    up_weight_whole = up_weight_whole[0]

    def spread(row_block):
        return placed_rows(row_block).reshape(owner_index, slot_capacity, model_width_value)

    arrived = lax.all_to_all(
        spread(tokens), "owner", split_axis=0, concat_axis=0, tiled=True
    ).reshape(owner_index * slot_capacity, model_width_value)
    hidden_state = lax.dot_general(
        arrived, down_full, (((1,), (1,)), ((), ())), preferred_element_type=jnp.float32
    ).astype(jnp.bfloat16)
    adapter_output = (
        adapter_scale * jnp.dot(hidden_state, up_weight_whole, preferred_element_type=jnp.float32)
    ).astype(jnp.bfloat16)
    hidden_state, adapter_output = (hidden_state, adapter_output)
    returned = lax.all_to_all(
        adapter_output.reshape(owner_index, slot_capacity, model_width_value),
        "owner",
        split_axis=0,
        concat_axis=0,
        tiled=True,
    )
    returned = returned.reshape(owner_index * slot_capacity, model_width_value)
    adapter_home_index = lax.dot_general(
        dispatch, returned, (((0,), (0,)), ((), ())), preferred_element_type=jnp.float32
    )
    shifted_index = residual.astype(jnp.float32) + adapter_home_index
    token_loss = jnp.mean(0.5 * shifted_index * shifted_index, axis=1)
    output_gradient = lax.all_to_all(
        spread(shifted_index.astype(jnp.bfloat16)), "owner", split_axis=0, concat_axis=0, tiled=True
    )
    output_gradient = output_gradient.reshape(owner_index * slot_capacity, model_width_value)
    up_gradient = adapter_scale * lax.dot_general(
        hidden_state, output_gradient, (((0,), (0,)), ((), ())), preferred_element_type=jnp.float32
    )
    hidden_gradient = (
        adapter_scale
        * lax.dot_general(
            output_gradient,
            up_weight_whole,
            (((1,), (1,)), ((), ())),
            preferred_element_type=jnp.float32,
        )
    ).astype(jnp.bfloat16)
    down_grad = lax.dot_general(
        hidden_gradient, arrived, (((0,), (0,)), ((), ())), preferred_element_type=jnp.float32
    )
    summed_down, summed_up = lax.psum((down_grad, up_gradient), "dp")
    offset = lax.axis_index("dp") * column_span
    down_share = lax.dynamic_slice_in_dim(summed_down, offset, column_span, 1)
    up_share = lax.dynamic_slice_in_dim(summed_up, offset, column_span, 1)
    down_update = adam_update(down_share, down_moment_first[0], down_moment_second[0])
    up_update = adam_update(up_share, up_moment_first[0], up_moment_second[0])
    return (down_update[None], up_update[None], token_loss)


def solution(mesh):
    return jax.shard_map(
        body,
        mesh=mesh,
        in_specs=(
            P(("dp", "owner"), None),
            P(("dp", "owner"), None),
            P(("dp", "owner"), None),
            P("owner", None, "dp"),
            P("owner", None, "dp"),
            P("owner", None, "dp"),
            P("owner", None, "dp"),
            P("owner", None, "dp"),
            P("owner", None, "dp"),
        ),
        out_specs=(P("owner", None, "dp"), P("owner", None, "dp"), P(("dp", "owner"))),
        check_vma=False,
    )
```

profile of v0, /device:TPU:6, one launch (start us, length us, event | category | flops | bytes accessed | tf_op | source)
XLA Modules:
  0.0 467.8 jit_solution(18413843679098739913)
XLA Ops:
  7.2 0.0 copy-start
  7.2 0.0 all-gather.3.cloned.1.call-start
  7.2 0.7 all-gather.3.cloned.1.call-update
  7.9 0.7 fusion.19
  8.7 0.2 reduce_window_sum.11
  8.8 0.8 select_reduce_fusion
  9.7 0.7 multiply_add_fusion
  10.3 0.0 copy-done
  10.3 2.6 convolution_convert_fusion.1
  12.9 4.9 %reshape.44 = bf16[32,6,8192]{2,1,0:T(8,128)(2,1)} reshape(bf16[192,8192]{1,0:T(8,128)(2,1)} %convolution_convert_fusion.1) | data formatting | bytes 6291456 | tf_op jit(solution)/shard_map/reshape | solution.py:54
  17.8 10.4 %all-to-all-start = ((bf16[32,6,8192]{2,1,0:T(8,128)(2,1)}), bf16[32,6,8192]{2,1,0:T(8,128)(2,1)}, u32[]{:S(2)}, u32[]{:S(2)}) async-start(bf16[32,6,8192]{2,1,0:T(8,128)(2,1)} %reshape.44), calls=%async_computation | async-start | bytes 8388608 | tf_op jit(solution)/shard_map/all_to_all | solution.py:56
  28.3 0.0 all-gather.5.cloned.1.call-start
  28.3 0.7 all-gather.5.cloned.1.call-update
  29.0 0.0 all-reduce.3.cloned.1.call-start
  29.1 50.0 %all-to-all-done = bf16[32,6,8192]{2,1,0:T(8,128)(2,1)} async-done(((bf16[32,6,8192]{2,1,0:T(8,128)(2,1)}), bf16[32,6,8192]{2,1,0:T(8,128)(2,1)}, u32[]{:S(2)}, u32[]{:S(2)}) %all-to-all-start) | async-done | bytes 3145760 | tf_op jit(solution)/shard_map/all_to_all | solution.py:56
  79.1 4.9 %reshape.45 = bf16[192,8192]{1,0:T(8,128)(2,1)} reshape(bf16[32,6,8192]{2,1,0:T(8,128)(2,1)} %all-to-all-done) | data formatting | bytes 6291456 | tf_op jit(solution)/shard_map/reshape | solution.py:58
  84.0 1.3 all-gather.3.cloned.1.call-done
  85.3 3.3 convolution_convert_fusion.2
  88.6 66.5 %all-gather.5.cloned.1.call-done = bf16[1,64,8192]{2,1,0:T(8,128)(2,1)} async-done(((bf16[1,64,512]{2,1,0:T(8,128)(2,1)}), bf16[1,64,8192]{2,1,0:T(8,128)(2,1)}) %all-gather.5.cloned.1.call-update) | async-done | bytes 1048592 | tf_op jit(solution)/shard_map/all_gather | solution.py:48
  155.0 3.9 fusion
  158.9 4.9 %reshape.46 = bf16[32,6,8192]{2,1,0:T(8,128)(2,1)} reshape(bf16[192,8192]{1,0:T(8,128)(2,1)} %fusion) | data formatting | bytes 6291456 | tf_op jit(solution)/shard_map/reshape | solution.py:67
  163.8 56.6 %all_to_all.15 = bf16[32,6,8192]{2,1,0:T(8,128)(2,1)} all-to-all(bf16[32,6,8192]{2,1,0:T(8,128)(2,1)} %reshape.46), channel_id=1, replica_groups=mesh['dp'=16,'owner'=32] {'owner'}, dimensions={0} | all-to-all | bytes 6291456 | tf_op jit(solution)/shard_map/all_to_all | solution.py:66
  220.4 4.9 %reshape.47 = bf16[192,8192]{1,0:T(8,128)(2,1)} reshape(bf16[32,6,8192]{2,1,0:T(8,128)(2,1)} %all_to_all.15) | data formatting | bytes 6291456 | tf_op jit(solution)/shard_map/reshape | solution.py:73
  225.2 3.9 fusion.1
  229.1 2.6 convolution_convert_fusion
  231.7 4.9 %reshape.48 = bf16[32,6,8192]{2,1,0:T(8,128)(2,1)} reshape(bf16[192,8192]{1,0:T(8,128)(2,1)} %convolution_convert_fusion) | data formatting | bytes 6291456 | tf_op jit(solution)/shard_map/reshape | solution.py:54
  236.6 55.2 %all_to_all.16 = bf16[32,6,8192]{2,1,0:T(8,128)(2,1)} all-to-all(bf16[32,6,8192]{2,1,0:T(8,128)(2,1)} %reshape.48), channel_id=1, replica_groups=mesh['dp'=16,'owner'=32] {'owner'}, dimensions={0} | all-to-all | bytes 6291456 | tf_op jit(solution)/shard_map/all_to_all | solution.py:79
  291.8 4.9 %reshape.49 = bf16[192,8192]{1,0:T(8,128)(2,1)} reshape(bf16[32,6,8192]{2,1,0:T(8,128)(2,1)} %all_to_all.16) | data formatting | bytes 6291456 | tf_op jit(solution)/shard_map/reshape | solution.py:82
  296.7 0.0 copy-start.1
  296.7 4.0 convolution_multiply_fusion.1
  300.7 0.0 copy-done.1
  300.7 6.5 %fusion.4 = f32[64,8192]{1,0:T(8,128)} fusion(bf16[192,8192]{1,0:T(8,128)(2,1)} %reshape.45, bf16[192,8192]{1,0:T(8,128)(2,1)} %reshape.49, bf16[1,64,8192]{2,1,0:T(8,128)(2,1)S(1)} %copy-done.1), kind=kOutput, calls=%fused_computation.12 | convolution fusion | flops 402677760 | bytes 9437184 | tf_op jit(solution)/shard_map/dot_general | solution.py:95
  307.2 0.0 copy-start.2
  307.2 0.0 copy-start.3
  307.2 0.0 copy-start.4
  307.2 0.0 copy-start.5
  307.2 0.0 all-reduce.3.cloned.1.call-update
  307.3 0.5 broadcast_multiply_fusion
  307.8 151.6 %all-reduce.3.cloned.1.call-done = (f32[64,8192]{1,0:T(8,128)}, f32[64,8192]{1,0:T(8,128)}) async-done(((f32[64,8192]{1,0:T(8,128)}, f32[64,8192]{1,0:T(8,128)}), (f32[64,8192]{1,0:T(8,128)}, f32[64,8192]{1,0:T(8,128)})) %all-reduce.3.cloned.1.call-update) | async-done | bytes 4194320 | tf_op jit(solution)/shard_map/psum | solution.py:98
  459.4 0.0 copy-done.2
  459.4 0.0 copy-done.3
  459.4 0.0 copy-done.4
  459.4 0.0 copy-done.5
  459.4 1.8 fusion.13
Async XLA Ops:
  7.2 3.2 copy-start
  7.2 78.1 %all-gather.3.cloned.1.call-start = ((), (), s32[]{:S(2)}) async-start(), calls=%async_computation.3 | async-start | bytes 1114112 | tf_op jit(solution)/shard_map/all_gather | solution.py:47
  17.8 61.2 %all-to-all-start = ((bf16[32,6,8192]{2,1,0:T(8,128)(2,1)}), bf16[32,6,8192]{2,1,0:T(8,128)(2,1)}, u32[]{:S(2)}, u32[]{:S(2)}) async-start(bf16[32,6,8192]{2,1,0:T(8,128)(2,1)} %reshape.44), calls=%async_computation | async-start | bytes 8388608 | tf_op jit(solution)/shard_map/all_to_all | solution.py:56
  28.3 126.8 %all-gather.5.cloned.1.call-start = ((), (), s32[]{:S(2)}) async-start(), calls=%async_computation.4 | async-start | bytes 1114112 | tf_op jit(solution)/shard_map/all_gather | solution.py:48
  29.0 430.4 %all-reduce.3.cloned.1.call-start = ((), (), s32[]{:S(2)}) async-start(), calls=%async_computation.5 | async-start | bytes 8388608 | tf_op jit(solution)/shard_map/psum | solution.py:98
  296.7 4.0 copy-start.1
  307.2 152.2 %copy-start.2 = (bf16[1,64,512]{2,1,0:T(8,128)(2,1)S(1)}, bf16[1,64,512]{2,1,0:T(8,128)(2,1)}, u32[]{:S(2)}) copy-start(bf16[1,64,512]{2,1,0:T(8,128)(2,1)} %param.15) | copy-start | bytes 196612
  307.2 152.2 %copy-start.3 = (bf16[1,64,512]{2,1,0:T(8,128)(2,1)S(1)}, bf16[1,64,512]{2,1,0:T(8,128)(2,1)}, u32[]{:S(2)}) copy-start(bf16[1,64,512]{2,1,0:T(8,128)(2,1)} %param.14) | copy-start | bytes 196612
  307.2 152.2 %copy-start.4 = (bf16[1,64,512]{2,1,0:T(8,128)(2,1)S(1)}, bf16[1,64,512]{2,1,0:T(8,128)(2,1)}, u32[]{:S(2)}) copy-start(bf16[1,64,512]{2,1,0:T(8,128)(2,1)} %param.17) | copy-start | bytes 196612
  307.2 152.2 %copy-start.5 = (bf16[1,64,512]{2,1,0:T(8,128)(2,1)S(1)}, bf16[1,64,512]{2,1,0:T(8,128)(2,1)}, u32[]{:S(2)}) copy-start(bf16[1,64,512]{2,1,0:T(8,128)(2,1)} %param.16) | copy-start | bytes 196612
Sparse Core Ops, SparseCore 0:
  10.1 75.1 all-gather.2
  87.4 67.6 all-gather.4
  307.4 151.9 all-reduce.2
where the time goes:
time: 469 us; the launch traced here: 468 us
  waiting for transfers between devices  271 us (58%)
  blocking collectives  112 us (24%)
  local copies, waits for them, and re-layouts  29.4 us (6%)
  matrix products  26.8 us (6%)
  between operations  13.8 us (3%)
  starting transfers between devices  10.5 us (2%)
  other arithmetic  4.76 us (1%)
    psum x1, waiting for transfers between devices, body(): summed_down, summed_up = lax.psum((down_grad, up_gradient), 'dp')  152 us
    all_gather x1, waiting for transfers between devices, body(): lax.all_gather(adapter_up_weight, 'dp', axis=2, tiled=True)  66.5 us
    all_to_all x1, blocking collectives, body(): lax.all_to_all(adapter_output.reshape(owner_index, slot_capacity, model_w...  56.6 us
    all_to_all x1, blocking collectives, body(): lax.all_to_all(spread(shifted_index.astype(jnp.bfloat16)), 'owner', split...  55.2 us
    all_to_all x1, waiting for transfers between devices, body(): lax.all_to_all(spread(tokens), 'owner', split_axis=0, concat_axis=0, tile...  50 us
    all_to_all x1, starting transfers between devices, body(): lax.all_to_all(spread(tokens), 'owner', split_axis=0, concat_axis=0, tile...  10.4 us
    reshape x2, local copies, waits for them, and re-layouts, spread(): placed_rows(row_block)  9.78 us
  transfers between devices with their start and end apart: 4, of which 4 were waited for; matrix products, arithmetic and copies ran while one was open for 4% of the time, Pallas kernels for 0%

commit v1 on v0

--- a/solution.py
+++ b/solution.py
@@ -5,6 +5,28 @@
 
 adapter_scale = 0.5
 adam_eps = 1e-08
+
+
+def laid_out(tiles, dim):
+    dims = list(tiles.shape[1:])
+    dims[dim] *= tiles.shape[0]
+    return jnp.moveaxis(tiles, 0, dim).reshape(dims)
+
+
+def ring_gather(x, axis, dim):
+    peers = lax.axis_size(axis)
+    pairs = [(i, (i + 1) % peers) for i in range(peers)]
+    back = [(b, a) for a, b in pairs]
+    lower, upper = ([], [])
+    for step in range(peers - 1):
+        if step % 2 == 0:
+            lower.append(lax.ppermute(lower[-1] if lower else x, axis, pairs))
+        else:
+            upper.append(lax.ppermute(upper[-1] if upper else x, axis, back))
+    blocks = jnp.stack([*lower[::-1], x, *upper])
+    shift = lax.axis_index(axis) - len(lower)
+    blocks = blocks[(jnp.arange(peers) - shift) % peers]
+    return laid_out(blocks, dim)
 
 
 def adam_update(grad, first, second):
@@ -45,7 +67,7 @@
 
     down_full, up_weight_whole = (
         lax.all_gather(adapter_down_weight, "dp", axis=2, tiled=True),
-        lax.all_gather(adapter_up_weight, "dp", axis=2, tiled=True),
+        ring_gather(adapter_up_weight, "dp", 2),
     )
     down_full = down_full[0]
     up_weight_whole = up_weight_whole[0]

time: 469 us -> 444 us (0.947)
  waiting for transfers between devices: 271 us -> 187 us
  starting transfers between devices: 10.5 us -> 61.8 us
  local copies, waits for them, and re-layouts: 29.4 us -> 36.8 us
    all_gather x1 -> x0, waiting for transfers between devices: 66.5 us -> none  [body(): lax.all_gather(adapter_up_weight, 'dp', axis=2, tiled=True)]
    ppermute x0 -> x15, starting transfers between devices: none -> 53.9 us  [the longest x7 36.5 us: ring_gather(): upper.append(lax.ppermute(upper[-1] if upper else x, axis, back))]
    all_to_all x1, waiting for transfers between devices: 50 us -> 23 us  [body(): lax.all_to_all(spread(tokens), 'owner', split_axis=0, concat_axis=0, tile...]
    ppermute x0 -> x15, waiting for transfers between devices: none -> 10.6 us  [the longest x8 10.6 us: ring_gather(): lower.append(lax.ppermute(lower[-1] if lower else x, axis, pairs))]
    unnamed x12 -> x38, local copies, waits for them, and re-layouts: 0.03 us -> 5.66 us
  transfers between devices with their start and end apart: 4 -> 18, of which waited for: 4 -> 5; matrix products, arithmetic and copies ran while one was open for 4% -> 5% of each run, Pallas kernels for 0% -> 0%
where the time goes in v1:
time: 444 us; the launch traced here: 443 us
  waiting for transfers between devices  187 us (42%)
  blocking collectives  113 us (25%)
  starting transfers between devices  61.8 us (14%)
  local copies, waits for them, and re-layouts  36.8 us (8%)
  matrix products  25.5 us (6%)
  between operations  14.5 us (3%)
  other arithmetic  4.78 us (1%)
    psum x1, waiting for transfers between devices, body(): summed_down, summed_up = lax.psum((down_grad, up_gradient), 'dp')  153 us
    all_to_all x1, blocking collectives, body(): lax.all_to_all(adapter_output.reshape(owner_index, slot_capacity, model_w...  57.5 us
    all_to_all x1, blocking collectives, body(): lax.all_to_all(spread(shifted_index.astype(jnp.bfloat16)), 'owner', split...  55.2 us
    ppermute x7, starting transfers between devices, ring_gather(): upper.append(lax.ppermute(upper[-1] if upper else x, axis, back))  36.5 us
    all_to_all x1, waiting for transfers between devices, body(): lax.all_to_all(spread(tokens), 'owner', split_axis=0, concat_axis=0, tile...  23 us
    ppermute x8, starting transfers between devices, ring_gather(): lower.append(lax.ppermute(lower[-1] if lower else x, axis, pairs))  17.4 us
    ppermute x8, waiting for transfers between devices, ring_gather(): lower.append(lax.ppermute(lower[-1] if lower else x, axis, pairs))  10.6 us
    reshape x2, local copies, waits for them, and re-layouts, spread(): placed_rows(row_block)  9.85 us
  transfers between devices with their start and end apart: 18, of which 5 were waited for; matrix products, arithmetic and copies ran while one was open for 5% of the time, Pallas kernels for 0%

profile of v1, /device:TPU:6, one launch (start us, length us, event | category | flops | bytes accessed | tf_op | source)
XLA Modules:
  0.0 442.6 jit_solution(14824861638663987256)
XLA Ops:
  7.2 4.0 collective-permute-start
  11.2 10.0 %collective-permute-done = bf16[1,64,512]{2,1,0:T(8,128)(2,1)S(1)} collective-permute-done((bf16[1,64,512]{2,1,0:T(8,128)(2,1)}, bf16[1,64,512]{2,1,0:T(8,128)(2,1)S(1)}, u32[]{:S(2)}, u32[]{:S(2)}) %collective-permute-start) | collective-permute-done | bytes 65568 | tf_op jit(solution)/shard_map/ppermute | solution.py:23
  21.2 1.9 collective-permute-start.1
  23.1 5.1 %collective-permute-start.8 = (bf16[1,64,512]{2,1,0:T(8,128)(2,1)}, bf16[1,64,512]{2,1,0:T(8,128)(2,1)S(1)}, u32[]{:S(2)}, u32[]{:S(2)}) collective-permute-start(bf16[1,64,512]{2,1,0:T(8,128)(2,1)} %param.13), channel_id=1, source_target_pairs={{32,0},{64,32},{96,64},{128,96},{160,128},{192,160},{224,192},{256... | collective-permute-start | bytes 196616 | tf_op jit(solution)/shard_map/ppermute | solution.py:25
  28.3 0.3 collective-permute-done.1
  28.6 1.9 collective-permute-start.2
  30.5 0.7 fusion.16
  31.4 5.1 %collective-permute-start.9 = (bf16[1,64,512]{2,1,0:T(8,128)(2,1)S(1)}, bf16[1,64,512]{2,1,0:T(8,128)(2,1)S(1)}, u32[]{:S(2)}, u32[]{:S(2)}) collective-permute-start(bf16[1,64,512]{2,1,0:T(8,128)(2,1)S(1)} %collective-permute-done.8), channel_id=1, source_target_pairs={{32,0},{64,32},{96,64},{128,96},{160,128},{192,160},{224,192},{256... | collective-permute-start | bytes 196616 | tf_op jit(solution)/shard_map/ppermute | solution.py:25
  36.6 1.9 collective-permute-start.3
  38.5 0.8 select_reduce_fusion
  39.3 5.1 %collective-permute-start.10 = (bf16[1,64,512]{2,1,0:T(8,128)(2,1)S(1)}, bf16[1,64,512]{2,1,0:T(8,128)(2,1)S(1)}, u32[]{:S(2)}, u32[]{:S(2)}) collective-permute-start(bf16[1,64,512]{2,1,0:T(8,128)(2,1)S(1)} %collective-permute-done.9), channel_id=1, source_target_pairs={{32,0},{64,32},{96,64},{128,96},{160,128},{192,160},{224,192},{256... | collective-permute-start | bytes 196616 | tf_op jit(solution)/shard_map/ppermute | solution.py:25
  44.5 1.9 collective-permute-start.4
  46.4 0.7 multiply_add_fusion
  47.1 5.1 %collective-permute-start.11 = (bf16[1,64,512]{2,1,0:T(8,128)(2,1)S(1)}, bf16[1,64,512]{2,1,0:T(8,128)(2,1)S(1)}, u32[]{:S(2)}, u32[]{:S(2)}) collective-permute-start(bf16[1,64,512]{2,1,0:T(8,128)(2,1)S(1)} %collective-permute-done.10), channel_id=1, source_target_pairs={{32,0},{64,32},{96,64},{128,96},{160,128},{192,160},{224,192},{256... | collective-permute-start | bytes 196616 | tf_op jit(solution)/shard_map/ppermute | solution.py:25
  52.2 1.9 collective-permute-start.5
  54.2 2.6 convolution_convert_fusion.1
  56.8 5.0 %reshape.93 = bf16[32,6,8192]{2,1,0:T(8,128)(2,1)} reshape(bf16[192,8192]{1,0:T(8,128)(2,1)} %convolution_convert_fusion.1) | data formatting | bytes 6291456 | tf_op jit(solution)/shard_map/reshape | solution.py:76
  61.8 7.8 %all-to-all-start = ((bf16[32,6,8192]{2,1,0:T(8,128)(2,1)}), bf16[32,6,8192]{2,1,0:T(8,128)(2,1)}, u32[]{:S(2)}, u32[]{:S(2)}) async-start(bf16[32,6,8192]{2,1,0:T(8,128)(2,1)} %reshape.93), calls=%async_computation | async-start | bytes 8388608 | tf_op jit(solution)/shard_map/all_to_all | solution.py:78
  69.7 5.1 %collective-permute-start.12 = (bf16[1,64,512]{2,1,0:T(8,128)(2,1)S(1)}, bf16[1,64,512]{2,1,0:T(8,128)(2,1)S(1)}, u32[]{:S(2)}, u32[]{:S(2)}) collective-permute-start(bf16[1,64,512]{2,1,0:T(8,128)(2,1)S(1)} %collective-permute-done.11), channel_id=1, source_target_pairs={{32,0},{64,32},{96,64},{128,96},{160,128},{192,160},{224,192},{256... | collective-permute-start | bytes 196616 | tf_op jit(solution)/shard_map/ppermute | solution.py:25
  74.8 1.9 collective-permute-start.6
  76.8 5.5 %collective-permute-start.13 = (bf16[1,64,512]{2,1,0:T(8,128)(2,1)S(1)}, bf16[1,64,512]{2,1,0:T(8,128)(2,1)S(1)}, u32[]{:S(2)}, u32[]{:S(2)}) collective-permute-start(bf16[1,64,512]{2,1,0:T(8,128)(2,1)S(1)} %collective-permute-done.12), channel_id=1, source_target_pairs={{32,0},{64,32},{96,64},{128,96},{160,128},{192,160},{224,192},{256... | collective-permute-start | bytes 196616 | tf_op jit(solution)/shard_map/ppermute | solution.py:25
  82.2 0.2 collective-permute-done.6
  82.5 1.9 collective-permute-start.7
  84.4 5.4 %collective-permute-start.14 = (bf16[1,64,512]{2,1,0:T(8,128)(2,1)S(1)}, bf16[1,64,512]{2,1,0:T(8,128)(2,1)S(1)}, u32[]{:S(2)}, u32[]{:S(2)}) collective-permute-start(bf16[1,64,512]{2,1,0:T(8,128)(2,1)S(1)} %collective-permute-done.13), channel_id=1, source_target_pairs={{32,0},{64,32},{96,64},{128,96},{160,128},{192,160},{224,192},{256... | collective-permute-start | bytes 196616 | tf_op jit(solution)/shard_map/ppermute | solution.py:25
  89.9 0.8 bitcast_dynamic-update-slice_fusion.13
  90.8 0.8 bitcast_dynamic-update-slice_fusion.12
  91.6 0.8 bitcast_dynamic-update-slice_fusion.11
  92.5 0.8 bitcast_dynamic-update-slice_fusion.4
  93.4 0.8 bitcast_dynamic-update-slice_fusion.3
  94.3 1.7 gather_fusion
  96.0 1.3 copy.13
  97.3 23.0 %all-to-all-done = bf16[32,6,8192]{2,1,0:T(8,128)(2,1)} async-done(((bf16[32,6,8192]{2,1,0:T(8,128)(2,1)}), bf16[32,6,8192]{2,1,0:T(8,128)(2,1)}, u32[]{:S(2)}, u32[]{:S(2)}) %all-to-all-start) | async-done | bytes 3145760 | tf_op jit(solution)/shard_map/all_to_all | solution.py:78
  120.3 5.0 %reshape.94 = bf16[192,8192]{1,0:T(8,128)(2,1)} reshape(bf16[32,6,8192]{2,1,0:T(8,128)(2,1)} %all-to-all-done) | data formatting | bytes 6291456 | tf_op jit(solution)/shard_map/reshape | solution.py:80
  125.3 3.3 convolution_convert_fusion.2
  128.6 2.7 fusion
  131.3 4.9 %reshape.95 = bf16[32,6,8192]{2,1,0:T(8,128)(2,1)} reshape(bf16[192,8192]{1,0:T(8,128)(2,1)} %fusion) | data formatting | bytes 6291456 | tf_op jit(solution)/shard_map/reshape | solution.py:89
  136.2 57.5 %all_to_all.15 = bf16[32,6,8192]{2,1,0:T(8,128)(2,1)} all-to-all(bf16[32,6,8192]{2,1,0:T(8,128)(2,1)} %reshape.95), channel_id=1, replica_groups=mesh['dp'=16,'owner'=32] {'owner'}, dimensions={0} | all-to-all | bytes 6291456 | tf_op jit(solution)/shard_map/all_to_all | solution.py:88
  193.7 4.9 %reshape.96 = bf16[192,8192]{1,0:T(8,128)(2,1)} reshape(bf16[32,6,8192]{2,1,0:T(8,128)(2,1)} %all_to_all.15) | data formatting | bytes 6291456 | tf_op jit(solution)/shard_map/reshape | solution.py:95
  198.6 3.8 fusion.1
  202.4 2.6 convolution_convert_fusion
  205.1 4.9 %reshape.97 = bf16[32,6,8192]{2,1,0:T(8,128)(2,1)} reshape(bf16[192,8192]{1,0:T(8,128)(2,1)} %convolution_convert_fusion) | data formatting | bytes 6291456 | tf_op jit(solution)/shard_map/reshape | solution.py:76
  209.9 55.2 %all_to_all.16 = bf16[32,6,8192]{2,1,0:T(8,128)(2,1)} all-to-all(bf16[32,6,8192]{2,1,0:T(8,128)(2,1)} %reshape.97), channel_id=1, replica_groups=mesh['dp'=16,'owner'=32] {'owner'}, dimensions={0} | all-to-all | bytes 6291456 | tf_op jit(solution)/shard_map/all_to_all | solution.py:101
  265.2 4.9 %reshape.98 = bf16[192,8192]{1,0:T(8,128)(2,1)} reshape(bf16[32,6,8192]{2,1,0:T(8,128)(2,1)} %all_to_all.16) | data formatting | bytes 6291456 | tf_op jit(solution)/shard_map/reshape | solution.py:104
  270.0 6.5 %fusion.4 = f32[64,8192]{1,0:T(8,128)} fusion(bf16[192,8192]{1,0:T(8,128)(2,1)} %reshape.94, bf16[192,8192]{1,0:T(8,128)(2,1)} %reshape.98, bf16[64,8192]{1,0:T(8,128)(2,1)S(1)} %bitcast.76), kind=kOutput, calls=%fused_computation.13 | convolution fusion | flops 402677760 | bytes 9437184 | tf_op jit(solution)/shard_map/dot_general | solution.py:117
  276.6 3.9 convolution_multiply_fusion.1
  280.5 0.5 broadcast_multiply_fusion
  281.1 152.9 %all-reduce.3.cloned.1.call-done = (f32[64,8192]{1,0:T(8,128)}, f32[64,8192]{1,0:T(8,128)}) async-done(((f32[64,8192]{1,0:T(8,128)}, f32[64,8192]{1,0:T(8,128)}), (f32[64,8192]{1,0:T(8,128)}, f32[64,8192]{1,0:T(8,128)})) %all-reduce.3.cloned.1.call-update) | async-done | bytes 4194320 | tf_op jit(solution)/shard_map/psum | solution.py:120
  434.0 1.8 fusion.10
  (53 shorter events, 0.5 us)
Async XLA Ops:
  7.2 47.0 %copy-start = (bf16[128,8192]{1,0:T(8,128)(2,1)S(1)}, bf16[128,8192]{1,0:T(8,128)(2,1)}, u32[]{:S(2)}) copy-start(bf16[128,8192]{1,0:T(8,128)(2,1)} %param.9) | copy-start | bytes 6291460
  7.2 118.1 %all-gather.2.cloned.1.call-start = ((), (), s32[]{:S(2)}) async-start(), calls=%async_computation.3 | async-start | bytes 1114112 | tf_op jit(solution)/shard_map/all_gather | solution.py:69
  7.2 14.0 %collective-permute-start = (bf16[1,64,512]{2,1,0:T(8,128)(2,1)}, bf16[1,64,512]{2,1,0:T(8,128)(2,1)S(1)}, u32[]{:S(2)}, u32[]{:S(2)}) collective-permute-start(bf16[1,64,512]{2,1,0:T(8,128)(2,1)} %param.13), channel_id=1, source_target_pairs={{0,32},{32,64},{64,96},{96,128},{128,160},{160,192},{192,224},{224... | collective-permute-start | bytes 196616 | tf_op jit(solution)/shard_map/ppermute | solution.py:23
  21.2 7.4 %collective-permute-start.1 = (bf16[1,64,512]{2,1,0:T(8,128)(2,1)S(1)}, bf16[1,64,512]{2,1,0:T(8,128)(2,1)S(1)}, u32[]{:S(2)}, u32[]{:S(2)}) collective-permute-start(bf16[1,64,512]{2,1,0:T(8,128)(2,1)S(1)} %collective-permute-done), channel_id=1, source_target_pairs={{0,32},{32,64},{64,96},{96,128},{128,160},{160,192},{192,224},{224... | collective-permute-start | bytes 196616 | tf_op jit(solution)/shard_map/ppermute | solution.py:23
  23.1 8.3 %collective-permute-start.8 = (bf16[1,64,512]{2,1,0:T(8,128)(2,1)}, bf16[1,64,512]{2,1,0:T(8,128)(2,1)S(1)}, u32[]{:S(2)}, u32[]{:S(2)}) collective-permute-start(bf16[1,64,512]{2,1,0:T(8,128)(2,1)} %param.13), channel_id=1, source_target_pairs={{32,0},{64,32},{96,64},{128,96},{160,128},{192,160},{224,192},{256... | collective-permute-start | bytes 196616 | tf_op jit(solution)/shard_map/ppermute | solution.py:25
  28.6 8.0 %collective-permute-start.2 = (bf16[1,64,512]{2,1,0:T(8,128)(2,1)S(1)}, bf16[1,64,512]{2,1,0:T(8,128)(2,1)S(1)}, u32[]{:S(2)}, u32[]{:S(2)}) collective-permute-start(bf16[1,64,512]{2,1,0:T(8,128)(2,1)S(1)} %collective-permute-done.1), channel_id=1, source_target_pairs={{0,32},{32,64},{64,96},{96,128},{128,160},{160,192},{192,224},{224... | collective-permute-start | bytes 196616 | tf_op jit(solution)/shard_map/ppermute | solution.py:23
  31.4 7.9 %collective-permute-start.9 = (bf16[1,64,512]{2,1,0:T(8,128)(2,1)S(1)}, bf16[1,64,512]{2,1,0:T(8,128)(2,1)S(1)}, u32[]{:S(2)}, u32[]{:S(2)}) collective-permute-start(bf16[1,64,512]{2,1,0:T(8,128)(2,1)S(1)} %collective-permute-done.8), channel_id=1, source_target_pairs={{32,0},{64,32},{96,64},{128,96},{160,128},{192,160},{224,192},{256... | collective-permute-start | bytes 196616 | tf_op jit(solution)/shard_map/ppermute | solution.py:25
  36.6 7.9 %collective-permute-start.3 = (bf16[1,64,512]{2,1,0:T(8,128)(2,1)S(1)}, bf16[1,64,512]{2,1,0:T(8,128)(2,1)S(1)}, u32[]{:S(2)}, u32[]{:S(2)}) collective-permute-start(bf16[1,64,512]{2,1,0:T(8,128)(2,1)S(1)} %collective-permute-done.2), channel_id=1, source_target_pairs={{0,32},{32,64},{64,96},{96,128},{128,160},{160,192},{192,224},{224... | collective-permute-start | bytes 196616 | tf_op jit(solution)/shard_map/ppermute | solution.py:23
  39.3 7.8 %collective-permute-start.10 = (bf16[1,64,512]{2,1,0:T(8,128)(2,1)S(1)}, bf16[1,64,512]{2,1,0:T(8,128)(2,1)S(1)}, u32[]{:S(2)}, u32[]{:S(2)}) collective-permute-start(bf16[1,64,512]{2,1,0:T(8,128)(2,1)S(1)} %collective-permute-done.9), channel_id=1, source_target_pairs={{32,0},{64,32},{96,64},{128,96},{160,128},{192,160},{224,192},{256... | collective-permute-start | bytes 196616 | tf_op jit(solution)/shard_map/ppermute | solution.py:25
  44.5 17.3 %copy-start.3 = (bf16[1,64,512]{2,1,0:T(8,128)(2,1)}, bf16[1,64,512]{2,1,0:T(8,128)(2,1)S(1)}, u32[]{:S(2)}) copy-start(bf16[1,64,512]{2,1,0:T(8,128)(2,1)S(1)} %collective-permute-done.3) | copy-start | bytes 196612
  44.5 7.7 %collective-permute-start.4 = (bf16[1,64,512]{2,1,0:T(8,128)(2,1)S(1)}, bf16[1,64,512]{2,1,0:T(8,128)(2,1)S(1)}, u32[]{:S(2)}, u32[]{:S(2)}) collective-permute-start(bf16[1,64,512]{2,1,0:T(8,128)(2,1)S(1)} %collective-permute-done.3), channel_id=1, source_target_pairs={{0,32},{32,64},{64,96},{96,128},{128,160},{160,192},{192,224},{224... | collective-permute-start | bytes 196616 | tf_op jit(solution)/shard_map/ppermute | solution.py:23
  47.1 14.7 %copy-start.2 = (bf16[1,64,512]{2,1,0:T(8,128)(2,1)}, bf16[1,64,512]{2,1,0:T(8,128)(2,1)S(1)}, u32[]{:S(2)}) copy-start(bf16[1,64,512]{2,1,0:T(8,128)(2,1)S(1)} %collective-permute-done.10) | copy-start | bytes 196612
  47.1 22.6 %collective-permute-start.11 = (bf16[1,64,512]{2,1,0:T(8,128)(2,1)S(1)}, bf16[1,64,512]{2,1,0:T(8,128)(2,1)S(1)}, u32[]{:S(2)}, u32[]{:S(2)}) collective-permute-start(bf16[1,64,512]{2,1,0:T(8,128)(2,1)S(1)} %collective-permute-done.10), channel_id=1, source_target_pairs={{32,0},{64,32},{96,64},{128,96},{160,128},{192,160},{224,192},{256... | collective-permute-start | bytes 196616 | tf_op jit(solution)/shard_map/ppermute | solution.py:25
  52.2 9.5 %copy-start.5 = (bf16[1,64,512]{2,1,0:T(8,128)(2,1)}, bf16[1,64,512]{2,1,0:T(8,128)(2,1)S(1)}, u32[]{:S(2)}) copy-start(bf16[1,64,512]{2,1,0:T(8,128)(2,1)S(1)} %collective-permute-done.4) | copy-start | bytes 196612
  52.2 22.6 %collective-permute-start.5 = (bf16[1,64,512]{2,1,0:T(8,128)(2,1)S(1)}, bf16[1,64,512]{2,1,0:T(8,128)(2,1)S(1)}, u32[]{:S(2)}, u32[]{:S(2)}) collective-permute-start(bf16[1,64,512]{2,1,0:T(8,128)(2,1)S(1)} %collective-permute-done.4), channel_id=1, source_target_pairs={{0,32},{32,64},{64,96},{96,128},{128,160},{160,192},{192,224},{224... | collective-permute-start | bytes 196616 | tf_op jit(solution)/shard_map/ppermute | solution.py:23
  61.8 30.7 %copy-start.1 = (bf16[1,64,512]{2,1,0:T(8,128)(2,1)S(1)}, bf16[1,64,512]{2,1,0:T(8,128)(2,1)}, u32[]{:S(2)}) copy-start(bf16[1,64,512]{2,1,0:T(8,128)(2,1)} %param.13) | copy-start | bytes 196612
  61.8 58.6 %all-to-all-start = ((bf16[32,6,8192]{2,1,0:T(8,128)(2,1)}), bf16[32,6,8192]{2,1,0:T(8,128)(2,1)}, u32[]{:S(2)}, u32[]{:S(2)}) async-start(bf16[32,6,8192]{2,1,0:T(8,128)(2,1)} %reshape.93), calls=%async_computation | async-start | bytes 8388608 | tf_op jit(solution)/shard_map/all_to_all | solution.py:78
  69.6 364.4 %all-reduce.3.cloned.1.call-start = ((), (), s32[]{:S(2)}) async-start(), calls=%async_computation.4 | async-start | bytes 8388608 | tf_op jit(solution)/shard_map/psum | solution.py:120
  69.7 20.2 %copy-start.4 = (bf16[1,64,512]{2,1,0:T(8,128)(2,1)}, bf16[1,64,512]{2,1,0:T(8,128)(2,1)S(1)}, u32[]{:S(2)}) copy-start(bf16[1,64,512]{2,1,0:T(8,128)(2,1)S(1)} %collective-permute-done.11) | copy-start | bytes 196612
  69.7 7.1 %collective-permute-start.12 = (bf16[1,64,512]{2,1,0:T(8,128)(2,1)S(1)}, bf16[1,64,512]{2,1,0:T(8,128)(2,1)S(1)}, u32[]{:S(2)}, u32[]{:S(2)}) collective-permute-start(bf16[1,64,512]{2,1,0:T(8,128)(2,1)S(1)} %collective-permute-done.11), channel_id=1, source_target_pairs={{32,0},{64,32},{96,64},{128,96},{160,128},{192,160},{224,192},{256... | collective-permute-start | bytes 196616 | tf_op jit(solution)/shard_map/ppermute | solution.py:25
  74.8 15.0 %copy-start.6 = (bf16[1,64,512]{2,1,0:T(8,128)(2,1)}, bf16[1,64,512]{2,1,0:T(8,128)(2,1)S(1)}, u32[]{:S(2)}) copy-start(bf16[1,64,512]{2,1,0:T(8,128)(2,1)S(1)} %collective-permute-done.5) | copy-start | bytes 196612
  74.8 7.6 %collective-permute-start.6 = (bf16[1,64,512]{2,1,0:T(8,128)(2,1)S(1)}, bf16[1,64,512]{2,1,0:T(8,128)(2,1)S(1)}, u32[]{:S(2)}, u32[]{:S(2)}) collective-permute-start(bf16[1,64,512]{2,1,0:T(8,128)(2,1)S(1)} %collective-permute-done.5), channel_id=1, source_target_pairs={{0,32},{32,64},{64,96},{96,128},{128,160},{160,192},{192,224},{224... | collective-permute-start | bytes 196616 | tf_op jit(solution)/shard_map/ppermute | solution.py:23
  76.8 7.6 %collective-permute-start.13 = (bf16[1,64,512]{2,1,0:T(8,128)(2,1)S(1)}, bf16[1,64,512]{2,1,0:T(8,128)(2,1)S(1)}, u32[]{:S(2)}, u32[]{:S(2)}) collective-permute-start(bf16[1,64,512]{2,1,0:T(8,128)(2,1)S(1)} %collective-permute-done.12), channel_id=1, source_target_pairs={{32,0},{64,32},{96,64},{128,96},{160,128},{192,160},{224,192},{256... | collective-permute-start | bytes 196616 | tf_op jit(solution)/shard_map/ppermute | solution.py:25
  82.5 7.4 %collective-permute-start.7 = (bf16[1,64,512]{2,1,0:T(8,128)(2,1)S(1)}, bf16[1,64,512]{2,1,0:T(8,128)(2,1)S(1)}, u32[]{:S(2)}, u32[]{:S(2)}) collective-permute-start(bf16[1,64,512]{2,1,0:T(8,128)(2,1)S(1)} %collective-permute-done.6), channel_id=1, source_target_pairs={{0,32},{32,64},{64,96},{96,128},{128,160},{160,192},{192,224},{224... | collective-permute-start | bytes 196616 | tf_op jit(solution)/shard_map/ppermute | solution.py:23
  84.4 9.9 %collective-permute-start.14 = (bf16[1,64,512]{2,1,0:T(8,128)(2,1)S(1)}, bf16[1,64,512]{2,1,0:T(8,128)(2,1)S(1)}, u32[]{:S(2)}, u32[]{:S(2)}) collective-permute-start(bf16[1,64,512]{2,1,0:T(8,128)(2,1)S(1)} %collective-permute-done.13), channel_id=1, source_target_pairs={{32,0},{64,32},{96,64},{128,96},{160,128},{192,160},{224,192},{256... | collective-permute-start | bytes 196616 | tf_op jit(solution)/shard_map/ppermute | solution.py:25
  280.5 153.4 %copy-start.7 = (bf16[1,64,512]{2,1,0:T(8,128)(2,1)S(1)}, bf16[1,64,512]{2,1,0:T(8,128)(2,1)}, u32[]{:S(2)}) copy-start(bf16[1,64,512]{2,1,0:T(8,128)(2,1)} %param.15) | copy-start | bytes 196612
  280.5 153.4 %copy-start.8 = (bf16[1,64,512]{2,1,0:T(8,128)(2,1)S(1)}, bf16[1,64,512]{2,1,0:T(8,128)(2,1)}, u32[]{:S(2)}) copy-start(bf16[1,64,512]{2,1,0:T(8,128)(2,1)} %param.14) | copy-start | bytes 196612
  280.5 153.4 %copy-start.9 = (bf16[1,64,512]{2,1,0:T(8,128)(2,1)S(1)}, bf16[1,64,512]{2,1,0:T(8,128)(2,1)}, u32[]{:S(2)}) copy-start(bf16[1,64,512]{2,1,0:T(8,128)(2,1)} %param.17) | copy-start | bytes 196612
  280.5 153.4 %copy-start.10 = (bf16[1,64,512]{2,1,0:T(8,128)(2,1)S(1)}, bf16[1,64,512]{2,1,0:T(8,128)(2,1)}, u32[]{:S(2)}) copy-start(bf16[1,64,512]{2,1,0:T(8,128)(2,1)} %param.16) | copy-start | bytes 196612
Sparse Core Ops, SparseCore 0:
  28.4 69.3 all-gather.1
  280.7 153.2 all-reduce.2
